TPU v7x, 32 devices: a whole 2x2x4 slice. The times are simulated.
32 devices in a mesh: scene: 2 (over x), view: 16 (over z, y, core).
Axes of the slice: x: 2, y: 2, z: 4, core: 2. Of those that a mesh axis runs over, the one named last changes fastest.
Arguments:
- src_feat: bfloat16 [32, 32, 8192], P(('scene', 'view')), parts along dimension 0, may hold values from -6 to 6
- ref_feat: bfloat16 [32, 32, 512], P(('scene', 'view')), parts along dimension 0, may hold values from -6 to 6
- weight_table: bfloat16 [4, 128, 512], replicated, may hold values from -0.5 to 0.5
- src_block: int32 [32, 64, 4], P(('scene', 'view')), parts along dimension 0, may hold values from 0 to 63
- table_index: int32 [32, 64, 4], P(('scene', 'view')), parts along dimension 0, may hold values from 0 to 3, each once within a row
- block_count: int32 [32, 64], P(('scene', 'view')), parts along dimension 0, may hold values from 0 to 4, as said below
- depth_plane: int32 [32, 64], P(('scene', 'view')), parts along dimension 0, may hold values from 0 to 63
- kern_one: bfloat16 [3, 3, 3, 8, 8], replicated, may hold values from -0.4375 to 0.4375
- kern_two: bfloat16 [3, 3, 3, 8], replicated, may hold values from -0.4375 to 0.4375
Outputs:
- depth_score: float32 [128, 64, 128], P(('scene', 'view')), parts along dimension 0
There are 2 independent parts, one for each index of `scene`. A program takes and returns all parts, laid end to end along the dimension named above; an argument that names none is the same for every part. Nothing has to cross between parts.
Inputs may be any that keep to these rules, and one draw needn't show every extreme that they name: `block_count`: each entry is the number of live block slots of a unit, 0 for an empty unit; the share of live units differs between source views. `table_index`: the 4 table indices of a unit are distinct.
All inputs are finite; a program needn't handle non-finite values.
Results may differ from a plain program's by a relative error of at most 0.019.
Values may be sent and summed in bfloat16 or wider, within the bound.
No kernel may reach another device: no remote copies, remote signals or barrier semaphores. Data moves between devices by JAX's collectives and lax.ppermute only.
A program may use at most 128 MiB of HBM per device.

v0:
```python
import jax
import jax.numpy as jnp
from jax import lax
from jax.sharding import PartitionSpec as P

GROUPS = 8
DEPTH = 64
TROWS = 4


def with_halo(block, sides, width):
    for axis, dim in sides:
        count = lax.axis_size(axis)
        forward = [(i, i + 1) for i in range(count - 1)]
        backward = [(target, source) for source, target in forward]
        low = lax.ppermute(
            lax.slice_in_dim(block, block.shape[dim] - width, None, axis=dim), axis, forward
        )
        high = lax.ppermute(lax.slice_in_dim(block, 0, width, axis=dim), axis, backward)
        block = jnp.concatenate([low, block, high], axis=dim)
    return block


def convolve_full(padded, kernel):
    rows_out = padded.shape[0] - 2
    depth_len = padded.shape[2]
    columns = padded.shape[3]
    framed = jnp.pad(padded, ((0, 0), (0, 0), (1, 1), (1, 1)))
    carried = jnp.zeros((rows_out, kernel.shape[-1], depth_len, columns), jnp.float32)
    for depth_off in range(3):
        for row_off in range(3):
            for col_off in range(3):
                window = framed[
                    row_off : row_off + rows_out,
                    :,
                    depth_off : depth_off + depth_len,
                    col_off : col_off + columns,
                ]
                carried = carried + jnp.einsum(
                    "rcdw,ce->redw",
                    window,
                    kernel[depth_off, row_off, col_off],
                    preferred_element_type=jnp.float32,
                )
    return carried


def convolve_final(padded, kernel):
    rows_out = padded.shape[0] - 2
    depth_len = padded.shape[2]
    columns = padded.shape[3]
    framed = jnp.pad(padded, ((0, 0), (0, 0), (1, 1), (1, 1)))
    carried = jnp.zeros((rows_out, depth_len, columns), jnp.float32)
    for depth_off in range(3):
        for row_off in range(3):
            for col_off in range(3):
                window = framed[
                    row_off : row_off + rows_out,
                    :,
                    depth_off : depth_off + depth_len,
                    col_off : col_off + columns,
                ]
                carried = carried + jnp.einsum(
                    "rcdw,c->rdw",
                    window,
                    kernel[depth_off, row_off, col_off],
                    preferred_element_type=jnp.float32,
                )
    return carried


def pad_rows(volume):
    return with_halo(volume, (("view", 0),), 1)


def body(
    src_feat,
    ref_feat,
    weight_table,
    src_block,
    table_index,
    block_count,
    depth_plane,
    kern_one,
    kern_two,
):
    owners = lax.axis_size("view")
    features = src_feat[0]
    channels, spix = features.shape
    slots, block_width, tpix = weight_table.shape
    blocks = features.reshape(channels, spix // block_width, block_width).transpose(1, 0, 2)
    units = src_block.shape[1]
    cap = units // owners
    counts = block_count[0]
    live_slot = jnp.arange(slots)[None, :] < counts[:, None]
    chosen = (
        (table_index[0][:, :, None] == jnp.arange(slots)[None, None, :]) & live_slot[:, :, None]
    ).astype(jnp.bfloat16)
    depth_code = jnp.where(counts > 0, depth_plane[0], -1).astype(jnp.bfloat16)
    unit_rounds = 8
    per_round = units // unit_rounds
    index_groups = src_block[0].reshape(unit_rounds, per_round, slots)
    chosen_groups = chosen.reshape(unit_rounds, per_round, slots, slots)
    group_size = channels // GROUPS
    ref_all = lax.all_to_all(
        jnp.broadcast_to(ref_feat, (owners,) + ref_feat.shape[1:]),
        "view",
        split_axis=0,
        concat_axis=0,
        tiled=True,
    )

    def resample(index_rows, chosen_rows):
        gathered = blocks[index_rows]
        arranged = jnp.einsum(
            "ujw,ujck->uwck", chosen_rows, gathered, preferred_element_type=jnp.float32
        ).astype(jnp.bfloat16)
        return jnp.einsum(
            "uwck,wkp->ucp", arranged, weight_table, preferred_element_type=jnp.float32
        ).astype(jnp.bfloat16)

    warped_all = lax.map(
        lambda packed: resample(packed[0], packed[1]), (index_groups, chosen_groups)
    ).reshape(owners, cap, channels, tpix)
    products = ref_all.astype(jnp.float32)[:, None] * warped_all.astype(jnp.float32)
    corr_all = (
        (products.reshape(units, GROUPS, group_size, tpix).sum(axis=2) * (GROUPS / channels))
        .astype(jnp.bfloat16)
        .reshape(units, GROUPS * tpix)
    )
    tag_lanes = jnp.broadcast_to(depth_code[:, None], (units, 128))
    payload = jnp.concatenate([corr_all, tag_lanes], axis=1)
    arriving = lax.all_to_all(
        payload.reshape(owners, cap, GROUPS * tpix + 128),
        "view",
        split_axis=0,
        concat_axis=0,
        tiled=True,
    ).reshape(owners * cap, GROUPS * tpix + 128)
    received = arriving[:, : GROUPS * tpix]
    depth_tags = arriving[:, GROUPS * tpix]
    onehot = (depth_tags[None, :] == jnp.arange(DEPTH).astype(jnp.bfloat16)[:, None]).astype(
        jnp.bfloat16
    )
    summed = jnp.dot(onehot, received, preferred_element_type=jnp.float32)
    tallies = jnp.sum(onehot.astype(jnp.float32), axis=1)
    cost_volume = (summed / jnp.maximum(tallies, 1.0)[:, None]).astype(jnp.bfloat16)
    columns = tpix // TROWS
    volume = cost_volume.reshape(DEPTH, GROUPS, TROWS, columns).transpose(2, 1, 0, 3)
    hidden = jax.nn.relu(convolve_full(pad_rows(volume), kern_one)).astype(jnp.bfloat16)
    scores = convolve_final(pad_rows(hidden), kern_two)
    return scores


def solution(mesh):
    in_specs = (
        P(("scene", "view"), None, None),
        P(("scene", "view"), None, None),
        P(),
        P(("scene", "view"), None, None),
        P(("scene", "view"), None, None),
        P(("scene", "view"), None),
        P(("scene", "view"), None),
        P(),
        P(),
    )
    out_specs = P(("scene", "view"), None, None)
    return jax.shard_map(body, mesh=mesh, in_specs=in_specs, out_specs=out_specs, check_vma=False)
```

profile of v0, /device:TPU:15, one launch (start us, length us, event | category | flops | bytes accessed | tf_op | source)
XLA Modules:
  0.0 115.5 jit_solution(5268535318414478130)
XLA Ops:
  0.0 1.7 %broadcast_in_dim.18 = bf16[16,32,512]{2,1,0:T(8,128)(2,1)} broadcast(bf16[32,512]{1,0:T(8,128)(2,1)} %bitcast.519), dimensions={1,2} | broadcast | bytes 557056 | tf_op jit(solution)/shard_map/broadcast_in_dim | solution.py:106
  1.7 6.7 %all-to-all-start = ((bf16[16,32,512]{2,1,0:T(8,128)(2,1)}), bf16[16,32,512]{2,1,0:T(8,128)(2,1)S(1)}, u32[]{:S(2)}, u32[]{:S(2)}) async-start(bf16[16,32,512]{2,1,0:T(8,128)(2,1)} %broadcast_in_dim.18), calls=%async_computation | async-start | bytes 1048576 | tf_op jit(solution)/shard_map/all_to_all | solution.py:105
  8.4 0.5 broadcast.200
  8.9 1.3 %reduce.9 = s32[64]{0:T(128)S(1)} reduce(s32[1,64]{1,0:T(1,128)} %param.16, s32[]{:T(128)} %broadcast.200), dimensions={0}, to_apply=%param.16.reduce_sub_computation.3 | reduce | bytes 516 | tf_op args[5]
  11.0 20.8 %while.10 = (s32[]{:T(128)}, bf16[8,8,32,512]{3,2,1,0:T(8,128)(2,1)S(1)}, bf16[8,8,4,4]{1,3,2,0:T(4,128)(2,1)S(1)}, s32[8,8,4]{1,0,2:T(8,128)S(1)}, bf16[64,32,1...) while((s32[]{:T(128)}, bf16[8,8,32,512]{3,2,1,0:T(8,128)(2,1)S(1)}, ...), condition=%wide.region_1.2_spmd, body=%wide.region_0.1_spmd.sunk | while | flops 135529568 | bytes 2103897 | solution.py:122
  11.2 0.6 gather_fusion
  12.2 1.3 %fusion.280 = bf16[8,8,32,512]{3,2,1,0:T(8,128)(2,1)S(1)} fusion(bf16[8,8,32,512]{3,2,1,0:T(8,128)(2,1)S(1)} %get-tuple-element.117, s32[]{:T(128)} %get-tuple-element.116, bf16[4,128,512]{2,1,0:T(8,128)(2,1)} %get-tuple-element.128, bf16[8,4,32,128]{3,1,2,0:T(4,128)(2,1)S(1)} %convolution_convert_fusion.2), kind=kOutput, calls=%fused_computation.5.clone.1 | convolution fusion | flops 134348800 | bytes 1048580 | tf_op jit(solution)/shard_map/while/body/eval_jaxpr/uwck,wkp->ucp/dot_general | solution.py:118
  13.8 0.6 gather_fusion
  14.8 1.3 %fusion.280 = bf16[8,8,32,512]{3,2,1,0:T(8,128)(2,1)S(1)} fusion(bf16[8,8,32,512]{3,2,1,0:T(8,128)(2,1)S(1)} %get-tuple-element.117, s32[]{:T(128)} %get-tuple-element.116, bf16[4,128,512]{2,1,0:T(8,128)(2,1)} %get-tuple-element.128, bf16[8,4,32,128]{3,1,2,0:T(4,128)(2,1)S(1)} %convolution_convert_fusion.2), kind=kOutput, calls=%fused_computation.5.clone.1 | convolution fusion | flops 134348800 | bytes 1048580 | tf_op jit(solution)/shard_map/while/body/eval_jaxpr/uwck,wkp->ucp/dot_general | solution.py:118
  16.4 0.6 gather_fusion
  17.4 1.3 %fusion.280 = bf16[8,8,32,512]{3,2,1,0:T(8,128)(2,1)S(1)} fusion(bf16[8,8,32,512]{3,2,1,0:T(8,128)(2,1)S(1)} %get-tuple-element.117, s32[]{:T(128)} %get-tuple-element.116, bf16[4,128,512]{2,1,0:T(8,128)(2,1)} %get-tuple-element.128, bf16[8,4,32,128]{3,1,2,0:T(4,128)(2,1)S(1)} %convolution_convert_fusion.2), kind=kOutput, calls=%fused_computation.5.clone.1 | convolution fusion | flops 134348800 | bytes 1048580 | tf_op jit(solution)/shard_map/while/body/eval_jaxpr/uwck,wkp->ucp/dot_general | solution.py:118
  19.0 0.6 gather_fusion
  20.1 1.3 %fusion.280 = bf16[8,8,32,512]{3,2,1,0:T(8,128)(2,1)S(1)} fusion(bf16[8,8,32,512]{3,2,1,0:T(8,128)(2,1)S(1)} %get-tuple-element.117, s32[]{:T(128)} %get-tuple-element.116, bf16[4,128,512]{2,1,0:T(8,128)(2,1)} %get-tuple-element.128, bf16[8,4,32,128]{3,1,2,0:T(4,128)(2,1)S(1)} %convolution_convert_fusion.2), kind=kOutput, calls=%fused_computation.5.clone.1 | convolution fusion | flops 134348800 | bytes 1048580 | tf_op jit(solution)/shard_map/while/body/eval_jaxpr/uwck,wkp->ucp/dot_general | solution.py:118
  21.6 0.6 gather_fusion
  22.7 1.3 %fusion.280 = bf16[8,8,32,512]{3,2,1,0:T(8,128)(2,1)S(1)} fusion(bf16[8,8,32,512]{3,2,1,0:T(8,128)(2,1)S(1)} %get-tuple-element.117, s32[]{:T(128)} %get-tuple-element.116, bf16[4,128,512]{2,1,0:T(8,128)(2,1)} %get-tuple-element.128, bf16[8,4,32,128]{3,1,2,0:T(4,128)(2,1)S(1)} %convolution_convert_fusion.2), kind=kOutput, calls=%fused_computation.5.clone.1 | convolution fusion | flops 134348800 | bytes 1048580 | tf_op jit(solution)/shard_map/while/body/eval_jaxpr/uwck,wkp->ucp/dot_general | solution.py:118
  24.2 0.6 gather_fusion
  25.3 1.3 %fusion.280 = bf16[8,8,32,512]{3,2,1,0:T(8,128)(2,1)S(1)} fusion(bf16[8,8,32,512]{3,2,1,0:T(8,128)(2,1)S(1)} %get-tuple-element.117, s32[]{:T(128)} %get-tuple-element.116, bf16[4,128,512]{2,1,0:T(8,128)(2,1)} %get-tuple-element.128, bf16[8,4,32,128]{3,1,2,0:T(4,128)(2,1)S(1)} %convolution_convert_fusion.2), kind=kOutput, calls=%fused_computation.5.clone.1 | convolution fusion | flops 134348800 | bytes 1048580 | tf_op jit(solution)/shard_map/while/body/eval_jaxpr/uwck,wkp->ucp/dot_general | solution.py:118
  26.8 0.6 gather_fusion
  27.9 1.3 %fusion.280 = bf16[8,8,32,512]{3,2,1,0:T(8,128)(2,1)S(1)} fusion(bf16[8,8,32,512]{3,2,1,0:T(8,128)(2,1)S(1)} %get-tuple-element.117, s32[]{:T(128)} %get-tuple-element.116, bf16[4,128,512]{2,1,0:T(8,128)(2,1)} %get-tuple-element.128, bf16[8,4,32,128]{3,1,2,0:T(4,128)(2,1)S(1)} %convolution_convert_fusion.2), kind=kOutput, calls=%fused_computation.5.clone.1 | convolution fusion | flops 134348800 | bytes 1048580 | tf_op jit(solution)/shard_map/while/body/eval_jaxpr/uwck,wkp->ucp/dot_general | solution.py:118
  29.4 0.6 gather_fusion
  30.5 1.3 %fusion.280 = bf16[8,8,32,512]{3,2,1,0:T(8,128)(2,1)S(1)} fusion(bf16[8,8,32,512]{3,2,1,0:T(8,128)(2,1)S(1)} %get-tuple-element.117, s32[]{:T(128)} %get-tuple-element.116, bf16[4,128,512]{2,1,0:T(8,128)(2,1)} %get-tuple-element.128, bf16[8,4,32,128]{3,1,2,0:T(4,128)(2,1)S(1)} %convolution_convert_fusion.2), kind=kOutput, calls=%fused_computation.5.clone.1 | convolution fusion | flops 134348800 | bytes 1048580 | tf_op jit(solution)/shard_map/while/body/eval_jaxpr/uwck,wkp->ucp/dot_general | solution.py:118
  31.8 3.0 %reshape.111 = f32[64,8,4,512]{3,2,1,0:T(4,128)} reshape(bf16[8,8,32,512]{3,2,1,0:T(8,128)(2,1)S(1)} %get-tuple-element.37) | data formatting | bytes 6291456 | tf_op jit(solution)/shard_map/convert_element_type | solution.py:125
  35.0 2.5 %mul.20 = f32[16,4,32,512]{3,2,1,0:T(8,128)} broadcast(bf16[16,32,512]{2,1,0:T(8,128)(2,1)S(1)} %all-to-all-done), dimensions={0,2,3} | broadcast | bytes 4718592 | tf_op jit(solution)/shard_map/mul | solution.py:125
  37.5 5.2 %mul.21 = f32[64,8,4,512]{3,2,1,0:T(4,128)} reshape(f32[16,4,32,512]{3,2,1,0:T(8,128)} %mul.20) | data formatting | bytes 8388608 | tf_op jit(solution)/shard_map/mul | solution.py:125
  42.7 7.4 %multiply_reduce_fusion = f32[64,8,512]{2,1,0:T(8,128)S(1)} fusion(f32[64,8,4,512]{3,2,1,0:T(4,128)} %mul.21, f32[64,8,4,512]{3,2,1,0:T(4,128)} %reshape.111), kind=kLoop, calls=%fused_computation.19 | loop fusion | flops 1835008 | bytes 9437184 | tf_op jit(solution)/shard_map/reduce_sum | solution.py:127
  50.2 0.4 convert_element_type.65
  50.7 1.0 pad_maximum_fusion
  51.7 6.0 %all-to-all-start.1 = ((bf16[16,4,4224]{2,1,0:T(4,128)(2,1)}), bf16[16,4,4224]{2,1,0:T(4,128)(2,1)S(1)}, u32[]{:S(2)}, u32[]{:S(2)}) async-start(bf16[16,4,4224]{2,1,0:T(4,128)(2,1)} %pad_maximum_fusion), calls=%async_computation.1 | async-start | bytes 1081344 | tf_op jit(solution)/shard_map/all_to_all | solution.py:133
  57.8 14.0 %all-to-all-done.1 = bf16[16,4,4224]{2,1,0:T(4,128)(2,1)S(1)} async-done(((bf16[16,4,4224]{2,1,0:T(4,128)(2,1)}), bf16[16,4,4224]{2,1,0:T(4,128)(2,1)S(1)}, u32[]{:S(2)}, u32[]{:S(2)}) %all-to-all-start.1) | async-done | bytes 540704 | tf_op jit(solution)/shard_map/all_to_all | solution.py:133
  72.5 0.4 reshape.110
  73.0 3.6 %collective-permute-start = (bf16[1,8,64,128]{3,1,2,0:T(8,128)(2,1)S(1)}, bf16[1,8,64,128]{3,1,2,0:T(8,128)(2,1)S(1)}, u32[]{:S(2)}, u32[]{:S(2)}) collective-permute-start(bf16[1,8,64,128]{3,1,2,0:T(8,128)(2,1)S(1)} %get-tuple-element.70), channel_id=1, source_target_pairs={{0,1},{1,2},{2,3},{3,4},{4,5},{5,6},{6,7},{7,8},{8,9},{9,10},{10,1... | collective-permute-start | bytes 393224 | tf_op jit(solution)/shard_map/ppermute | solution.py:16
  76.6 2.1 %collective-permute-start.1 = (bf16[1,8,64,128]{3,1,2,0:T(8,128)(2,1)S(1)}, bf16[1,8,64,128]{3,1,2,0:T(8,128)(2,1)S(1)}, u32[]{:S(2)}, u32[]{:S(2)}) collective-permute-start(bf16[1,8,64,128]{3,1,2,0:T(8,128)(2,1)S(1)} %get-tuple-element.71), channel_id=1, source_target_pairs={{1,0},{2,1},{3,2},{4,3},{5,4},{6,5},{7,6},{8,7},{9,8},{10,9},{11,1... | collective-permute-start | bytes 393224 | tf_op jit(solution)/shard_map/ppermute | solution.py:19
  79.1 4.7 %collective-permute-done.1 = bf16[1,8,64,128]{3,1,2,0:T(8,128)(2,1)S(1)} collective-permute-done((bf16[1,8,64,128]{3,1,2,0:T(8,128)(2,1)S(1)}, bf16[1,8,64,128]{3,1,2,0:T(8,128)(2,1)S(1)}, u32[]{:S(2)}, u32[]{:S(2)}) %collective-permute-start.1) | collective-permute-done | bytes 131104 | tf_op jit(solution)/shard_map/ppermute | solution.py:19
  83.8 1.5 %fusion.17 = bf16[6,8,66,130]{3,1,2,0:T(8,128)(2,1)S(1)} fusion(bf16[1,8,64,128]{3,1,2,0:T(8,128)(2,1)S(1)} %collective-permute-done.1, bf16[4,8,64,128]{3,1,2,0:T(8,128)(2,1)S(1)} %bitcast.485, bf16[1,8,64,128]{3,1,2,0:T(8,128)(2,1)S(1)} %collective-permute-done), kind=kLoop, calls=%fused_computation.32 | loop fusion | flops 7824960 | bytes 1610112 | tf_op jit(solution)/shard_map/concatenate | solution.py:20
  85.7 0.4 fusion.124
  86.4 0.4 fusion.128
  87.4 0.4 fusion.134
  87.8 0.4 fusion.136
  90.6 0.4 convolution_bitcast_fusion.4
  91.7 0.4 convolution_bitcast_fusion.7
  92.1 0.4 convolution_bitcast_fusion.8
  93.5 0.8 fusion.42
  94.7 0.8 fusion.44
  95.5 1.9 %collective-permute-start.2 = (bf16[1,8,64,128]{3,1,2,0:T(8,128)(2,1)S(1)}, bf16[1,8,64,128]{3,1,2,0:T(8,128)(2,1)S(1)}, u32[]{:S(2)}, u32[]{:S(2)}) collective-permute-start(bf16[1,8,64,128]{3,1,2,0:T(8,128)(2,1)S(1)} %get-tuple-element.68), channel_id=1, source_target_pairs={{0,1},{1,2},{2,3},{3,4},{4,5},{5,6},{6,7},{7,8},{8,9},{9,10},{10,1... | collective-permute-start | bytes 393224 | tf_op jit(solution)/shard_map/ppermute | solution.py:16
  97.4 2.6 %collective-permute-start.3 = (bf16[1,8,64,128]{3,1,2,0:T(8,128)(2,1)S(1)}, bf16[1,8,64,128]{3,1,2,0:T(8,128)(2,1)S(1)}, u32[]{:S(2)}, u32[]{:S(2)}) collective-permute-start(bf16[1,8,64,128]{3,1,2,0:T(8,128)(2,1)S(1)} %get-tuple-element.69), channel_id=1, source_target_pairs={{1,0},{2,1},{3,2},{4,3},{5,4},{6,5},{7,6},{8,7},{9,8},{10,9},{11,1... | collective-permute-start | bytes 393224 | tf_op jit(solution)/shard_map/ppermute | solution.py:19
  100.4 4.2 %collective-permute-done.3 = bf16[1,8,64,128]{3,1,2,0:T(8,128)(2,1)S(1)} collective-permute-done((bf16[1,8,64,128]{3,1,2,0:T(8,128)(2,1)S(1)}, bf16[1,8,64,128]{3,1,2,0:T(8,128)(2,1)S(1)}, u32[]{:S(2)}, u32[]{:S(2)}) %collective-permute-start.3) | collective-permute-done | bytes 131104 | tf_op jit(solution)/shard_map/ppermute | solution.py:19
  104.6 1.5 %select_maximum_fusion = bf16[6,8,66,130]{3,1,2,0:T(8,128)(2,1)S(1)} fusion(bf16[1,8,64,128]{3,1,2,0:T(8,128)(2,1)S(1)} %collective-permute-done.3, bf16[4,8,64,128]{3,1,2,0:T(8,128)(2,1)S(1)} %fusion.44, bf16[1,8,64,128]{3,1,2,0:T(8,128)(2,1)S(1)} %collective-permute-done.2), kind=kLoop, calls=%fused_computation.23 | loop fusion | flops 7824960 | bytes 1610112 | tf_op jit(solution)/shard_map/concatenate | solution.py:20
  114.6 0.9 add_add_fusion
  (148 shorter events, 21.7 us)
Async XLA Ops:
  0.0 10.3 %copy-start.3 = (s32[1,64,4]{1,2,0:T(4,128)S(1)}, s32[1,64,4]{1,2,0:T(4,128)}, u32[]{:S(2)}) copy-start(s32[1,64,4]{1,2,0:T(4,128)} %param.15) | copy-start | bytes 3076
  0.0 10.4 %copy-start = (bf16[1,32,8192]{2,1,0:T(8,128)(2,1)S(1)}, bf16[1,32,8192]{2,1,0:T(8,128)(2,1)}, u32[]{:S(2)}) copy-start(bf16[1,32,8192]{2,1,0:T(8,128)(2,1)} %param.11) | copy-start | bytes 1572868
  1.7 9.2 %copy-start.4 = (s32[1,64,4]{1,2,0:T(4,128)S(1)}, s32[1,64,4]{1,2,0:T(4,128)}, u32[]{:S(2)}) copy-start(s32[1,64,4]{1,2,0:T(4,128)} %param.14) | copy-start | bytes 3076
  1.7 33.3 %all-to-all-start = ((bf16[16,32,512]{2,1,0:T(8,128)(2,1)}), bf16[16,32,512]{2,1,0:T(8,128)(2,1)S(1)}, u32[]{:S(2)}, u32[]{:S(2)}) async-start(bf16[16,32,512]{2,1,0:T(8,128)(2,1)} %broadcast_in_dim.18), calls=%async_computation | async-start | bytes 1048576 | tf_op jit(solution)/shard_map/all_to_all | solution.py:105
  31.8 3.0 %copy-start.5 = (s32[1,64]{1,0:T(1,128)S(1)}, s32[1,64]{1,0:T(1,128)}, u32[]{:S(2)}) copy-start(s32[1,64]{1,0:T(1,128)} %param.17) | copy-start | bytes 772
  31.8 3.0 %copy-start.6 = (s32[1,64]{1,0:T(1,128)S(1)}, s32[1,64]{1,0:T(1,128)}, u32[]{:S(2)}) copy-start(s32[1,64]{1,0:T(1,128)} %param.16) | copy-start | bytes 772
  51.7 20.0 %all-to-all-start.1 = ((bf16[16,4,4224]{2,1,0:T(4,128)(2,1)}), bf16[16,4,4224]{2,1,0:T(4,128)(2,1)S(1)}, u32[]{:S(2)}, u32[]{:S(2)}) async-start(bf16[16,4,4224]{2,1,0:T(4,128)(2,1)} %pad_maximum_fusion), calls=%async_computation.1 | async-start | bytes 1081344 | tf_op jit(solution)/shard_map/all_to_all | solution.py:133
  72.5 6.2 %copy-start.2 = (bf16[3,3,3,8,8]{4,3,2,1,0:T(8,128)(2,1)S(1)}, bf16[3,3,3,8,8]{4,3,2,1,0:T(8,128)(2,1)}, u32[]{:S(2)}) copy-start(bf16[3,3,3,8,8]{4,3,2,1,0:T(8,128)(2,1)} %param.18) | copy-start | bytes 10372
  73.0 6.1 %collective-permute-start = (bf16[1,8,64,128]{3,1,2,0:T(8,128)(2,1)S(1)}, bf16[1,8,64,128]{3,1,2,0:T(8,128)(2,1)S(1)}, u32[]{:S(2)}, u32[]{:S(2)}) collective-permute-start(bf16[1,8,64,128]{3,1,2,0:T(8,128)(2,1)S(1)} %get-tuple-element.70), channel_id=1, source_target_pairs={{0,1},{1,2},{2,3},{3,4},{4,5},{5,6},{6,7},{7,8},{8,9},{9,10},{10,1... | collective-permute-start | bytes 393224 | tf_op jit(solution)/shard_map/ppermute | solution.py:16
  76.6 7.2 %collective-permute-start.1 = (bf16[1,8,64,128]{3,1,2,0:T(8,128)(2,1)S(1)}, bf16[1,8,64,128]{3,1,2,0:T(8,128)(2,1)S(1)}, u32[]{:S(2)}, u32[]{:S(2)}) collective-permute-start(bf16[1,8,64,128]{3,1,2,0:T(8,128)(2,1)S(1)} %get-tuple-element.71), channel_id=1, source_target_pairs={{1,0},{2,1},{3,2},{4,3},{5,4},{6,5},{7,6},{8,7},{9,8},{10,9},{11,1... | collective-permute-start | bytes 393224 | tf_op jit(solution)/shard_map/ppermute | solution.py:19
  94.6 5.4 %copy-start.1 = (bf16[3,3,3,8]{3,2,1,0:T(4,128)(2,1)S(1)}, bf16[3,3,3,8]{3,2,1,0:T(4,128)(2,1)}, u32[]{:S(2)}) copy-start(bf16[3,3,3,8]{3,2,1,0:T(4,128)(2,1)} %param.19) | copy-start | bytes 1300
  95.5 4.9 %collective-permute-start.2 = (bf16[1,8,64,128]{3,1,2,0:T(8,128)(2,1)S(1)}, bf16[1,8,64,128]{3,1,2,0:T(8,128)(2,1)S(1)}, u32[]{:S(2)}, u32[]{:S(2)}) collective-permute-start(bf16[1,8,64,128]{3,1,2,0:T(8,128)(2,1)S(1)} %get-tuple-element.68), channel_id=1, source_target_pairs={{0,1},{1,2},{2,3},{3,4},{4,5},{5,6},{6,7},{7,8},{8,9},{9,10},{10,1... | collective-permute-start | bytes 393224 | tf_op jit(solution)/shard_map/ppermute | solution.py:16
  97.4 7.2 %collective-permute-start.3 = (bf16[1,8,64,128]{3,1,2,0:T(8,128)(2,1)S(1)}, bf16[1,8,64,128]{3,1,2,0:T(8,128)(2,1)S(1)}, u32[]{:S(2)}, u32[]{:S(2)}) collective-permute-start(bf16[1,8,64,128]{3,1,2,0:T(8,128)(2,1)S(1)} %get-tuple-element.69), channel_id=1, source_target_pairs={{1,0},{2,1},{3,2},{4,3},{5,4},{6,5},{7,6},{8,7},{9,8},{10,9},{11,1... | collective-permute-start | bytes 393224 | tf_op jit(solution)/shard_map/ppermute | solution.py:19
where the time goes:
time: 116 us; the launch traced here: 115 us
  matrix products  32.3 us (28%)
  starting transfers between devices  23 us (20%)
  waiting for transfers between devices  22.9 us (20%)
  local copies, waits for them, and re-layouts  22.2 us (19%)
  other arithmetic  14 us (12%)
    all_to_all x1, waiting for transfers between devices, body(): lax.all_to_all(payload.reshape(owners, cap, GROUPS * tpix + 128), 'view',...  14 us
    dot_general x8, matrix products, resample(): jnp.einsum('uwck,wkp->ucp', arranged, weight_table, preferred_element_typ...  10.7 us
    dot_general x27, matrix products, convolve_full(): jnp.einsum('rcdw,ce->redw', window, kernel[depth_off, row_off, col_off],...  10.4 us
    ppermute x2, waiting for transfers between devices, with_halo(): lax.ppermute(lax.slice_in_dim(block, 0, width, axis=dim), axis, backward)  8.95 us
    dot_general x27, matrix products, convolve_final(): jnp.einsum('rcdw,c->rdw', window, kernel[depth_off, row_off, col_off], pr...  8.64 us
    mul x2, local copies, waits for them, and re-layouts, body(): ref_all.astype(jnp.float32)[:, None] * warped_all.astype(jnp.float32)  7.69 us
    reduce_sum x1, other arithmetic, body(): products.reshape(units, GROUPS, group_size, tpix).sum(axis=2)  7.41 us
    all_to_all x1, starting transfers between devices, body(): lax.all_to_all(jnp.broadcast_to(ref_feat, (owners,) + ref_feat.shape[1:])...  6.69 us
  transfers between devices with their start and end apart: 6, of which 3 were waited for; matrix products, arithmetic and copies ran while one was open for 23% of the time, Pallas kernels for 0%

commit v1 on v0

--- a/solution.py
+++ b/solution.py
@@ -6,6 +6,34 @@
 GROUPS = 8
 DEPTH = 64
 TROWS = 4
+
+
+def close_marks(arr_in, ndim_at, here_x):
+    s_next, passed = (arr_in.shape[:ndim_at], arr_in.shape[ndim_at + 1 :])
+    mixed_arr = arr_in.reshape(*s_next, here_x, -1, *passed)
+    return jnp.moveaxis(mixed_arr, ndim_at, 0)
+
+
+def _drive_steps_all(chunk, dim_i):
+    chunk = jnp.moveaxis(chunk, 0, dim_i)
+    r2 = chunk.shape
+    return chunk.reshape(*r2[:dim_i], r2[dim_i] * r2[dim_i + 1], *r2[dim_i + 2 :])
+
+
+def threads_carry(x_in, ax_name, local_values, x_local):
+    z2 = lax.axis_size(ax_name)
+    inter = lax.axis_index(ax_name)
+    v1, big = (z2, inter)
+    arr_out = close_marks(x_in, local_values, v1)
+    heard = arr_out
+    for to_i in range(1, v1):
+        opened, top = ((big + to_i) % v1, (big - to_i) % v1)
+        t_next = lax.dynamic_index_in_dim(arr_out, opened, 0)
+        carry_out = lax.ppermute(
+            t_next, axis_name=ax_name, perm=[(p, (p + to_i) % v1) for p in range(v1)]
+        )
+        heard = lax.dynamic_update_slice_in_dim(heard, carry_out, top, axis=0)
+    return _drive_steps_all(heard, x_local)
 
 
 def with_halo(block, sides, width):
@@ -102,12 +130,8 @@
     index_groups = src_block[0].reshape(unit_rounds, per_round, slots)
     chosen_groups = chosen.reshape(unit_rounds, per_round, slots, slots)
     group_size = channels // GROUPS
-    ref_all = lax.all_to_all(
-        jnp.broadcast_to(ref_feat, (owners,) + ref_feat.shape[1:]),
-        "view",
-        split_axis=0,
-        concat_axis=0,
-        tiled=True,
+    ref_all = threads_carry(
+        jnp.broadcast_to(ref_feat, (owners,) + ref_feat.shape[1:]), "view", 0, 0
     )
 
     def resample(index_rows, chosen_rows):

time: 116 us -> 134 us (1.16)
  starting transfers between devices: 23 us -> 37.2 us
  waiting for transfers between devices: 22.9 us -> 27.1 us
    ppermute x0 -> x15, starting transfers between devices: none -> 20.6 us  [threads_carry(): lax.ppermute(t_next, axis_name=ax_name, perm=[(p, (p + to_i) % v1) for p...]
    all_to_all x1 -> x0, starting transfers between devices: 6.69 us -> none  [body(): lax.all_to_all(jnp.broadcast_to(ref_feat, (owners,) + ref_feat.shape[1:])...]
    ppermute x0 -> x15, waiting for transfers between devices: none -> 4.17 us  [threads_carry(): lax.ppermute(t_next, axis_name=ax_name, perm=[(p, (p + to_i) % v1) for p...]
    broadcast_in_dim x1 -> x0, local copies, waits for them, and re-layouts: 1.67 us -> none  [body(): jnp.broadcast_to(ref_feat, (owners,) + ref_feat.shape[1:])]
  transfers between devices with their start and end apart: 6 -> 20, of which waited for: 3 -> 6; matrix products, arithmetic and copies ran while one was open for 23% -> 20% of each run, Pallas kernels for 0% -> 0%
where the time goes in v1:
time: 134 us; the launch traced here: 133 us
  starting transfers between devices  37.2 us (28%)
  matrix products  32.4 us (24%)
  waiting for transfers between devices  27.1 us (20%)
  local copies, waits for them, and re-layouts  21.7 us (16%)
  other arithmetic  13.3 us (10%)
    ppermute x15, starting transfers between devices, threads_carry(): lax.ppermute(t_next, axis_name=ax_name, perm=[(p, (p + to_i) % v1) for p...  20.6 us
    all_to_all x1, waiting for transfers between devices, body(): lax.all_to_all(payload.reshape(owners, cap, GROUPS * tpix + 128), 'view',...  14 us
    dot_general x8, matrix products, resample(): jnp.einsum('uwck,wkp->ucp', arranged, weight_table, preferred_element_typ...  10.7 us
    dot_general x27, matrix products, convolve_full(): jnp.einsum('rcdw,ce->redw', window, kernel[depth_off, row_off, col_off],...  10.5 us
    ppermute x2, waiting for transfers between devices, with_halo(): lax.ppermute(lax.slice_in_dim(block, 0, width, axis=dim), axis, backward)  8.95 us
    dot_general x27, matrix products, convolve_final(): jnp.einsum('rcdw,c->rdw', window, kernel[depth_off, row_off, col_off], pr...  8.64 us
    mul x2, local copies, waits for them, and re-layouts, body(): ref_all.astype(jnp.float32)[:, None] * warped_all.astype(jnp.float32)  7.75 us
    reduce_sum x1, other arithmetic, body(): products.reshape(units, GROUPS, group_size, tpix).sum(axis=2)  7.32 us
  transfers between devices with their start and end apart: 20, of which 6 were waited for; matrix products, arithmetic and copies ran while one was open for 20% of the time, Pallas kernels for 0%

profile of v1, /device:TPU:15, one launch (start us, length us, event | category | flops | bytes accessed | tf_op | source)
XLA Modules:
  0.0 133.3 jit_solution(7074844341282557759)
XLA Ops:
  0.0 1.9 %collective-permute-start = (bf16[1,1,32,512]{3,2,1,0:T(8,128)(2,1)}, bf16[1,1,32,512]{3,2,1,0:T(8,128)(2,1)S(1)}, u32[]{:S(2)}, u32[]{:S(2)}) collective-permute-start(bf16[1,1,32,512]{3,2,1,0:T(8,128)(2,1)} %bitcast.550), channel_id=1, source_target_pairs={{0,1},{1,2},{2,3},{3,4},{4,5},{5,6},{6,7},{7,8},{8,9},{9,10},{10,1... | collective-permute-start | bytes 98312 | tf_op jit(solution)/shard_map/ppermute | solution.py:32
  1.9 1.2 collective-permute-start.1
  3.5 0.9 collective-permute-start.3
  4.4 2.7 %collective-permute-start.4 = (bf16[1,1,32,512]{3,2,1,0:T(8,128)(2,1)}, bf16[1,1,32,512]{3,2,1,0:T(8,128)(2,1)S(1)}, u32[]{:S(2)}, u32[]{:S(2)}) collective-permute-start(bf16[1,1,32,512]{3,2,1,0:T(8,128)(2,1)} %bitcast.554), channel_id=1, source_target_pairs={{0,5},{1,6},{2,7},{3,8},{4,9},{5,10},{6,11},{7,12},{8,13},{9,14},{... | collective-permute-start | bytes 98312 | tf_op jit(solution)/shard_map/ppermute | solution.py:32
  7.1 1.2 copy.255
  9.2 0.7 reduce.9
  10.1 20.8 %while.10 = (s32[]{:T(128)}, bf16[8,8,32,512]{3,2,1,0:T(8,128)(2,1)S(1)}, bf16[8,8,4,4]{1,3,2,0:T(4,128)(2,1)S(1)}, s32[8,8,4]{1,0,2:T(8,128)S(1)}, bf16[64,32,1...) while((s32[]{:T(128)}, bf16[8,8,32,512]{3,2,1,0:T(8,128)(2,1)S(1)}, ...), condition=%wide.region_1.2_spmd, body=%wide.region_0.1_spmd.sunk | while | flops 135529568 | bytes 2103897 | solution.py:146
  10.4 0.6 gather_fusion
  11.4 1.3 %fusion.280 = bf16[8,8,32,512]{3,2,1,0:T(8,128)(2,1)S(1)} fusion(bf16[8,8,32,512]{3,2,1,0:T(8,128)(2,1)S(1)} %get-tuple-element.117, s32[]{:T(128)} %get-tuple-element.116, bf16[4,128,512]{2,1,0:T(8,128)(2,1)} %get-tuple-element.128, bf16[8,4,32,128]{3,1,2,0:T(4,128)(2,1)S(1)} %convolution_convert_fusion.2), kind=kOutput, calls=%fused_computation.5.clone.1 | convolution fusion | flops 134348800 | bytes 1048580 | tf_op jit(solution)/shard_map/while/body/eval_jaxpr/uwck,wkp->ucp/dot_general | solution.py:142
  13.0 0.6 gather_fusion
  14.0 1.3 %fusion.280 = bf16[8,8,32,512]{3,2,1,0:T(8,128)(2,1)S(1)} fusion(bf16[8,8,32,512]{3,2,1,0:T(8,128)(2,1)S(1)} %get-tuple-element.117, s32[]{:T(128)} %get-tuple-element.116, bf16[4,128,512]{2,1,0:T(8,128)(2,1)} %get-tuple-element.128, bf16[8,4,32,128]{3,1,2,0:T(4,128)(2,1)S(1)} %convolution_convert_fusion.2), kind=kOutput, calls=%fused_computation.5.clone.1 | convolution fusion | flops 134348800 | bytes 1048580 | tf_op jit(solution)/shard_map/while/body/eval_jaxpr/uwck,wkp->ucp/dot_general | solution.py:142
  15.6 0.6 gather_fusion
  16.6 1.3 %fusion.280 = bf16[8,8,32,512]{3,2,1,0:T(8,128)(2,1)S(1)} fusion(bf16[8,8,32,512]{3,2,1,0:T(8,128)(2,1)S(1)} %get-tuple-element.117, s32[]{:T(128)} %get-tuple-element.116, bf16[4,128,512]{2,1,0:T(8,128)(2,1)} %get-tuple-element.128, bf16[8,4,32,128]{3,1,2,0:T(4,128)(2,1)S(1)} %convolution_convert_fusion.2), kind=kOutput, calls=%fused_computation.5.clone.1 | convolution fusion | flops 134348800 | bytes 1048580 | tf_op jit(solution)/shard_map/while/body/eval_jaxpr/uwck,wkp->ucp/dot_general | solution.py:142
  18.2 0.6 gather_fusion
  19.2 1.3 %fusion.280 = bf16[8,8,32,512]{3,2,1,0:T(8,128)(2,1)S(1)} fusion(bf16[8,8,32,512]{3,2,1,0:T(8,128)(2,1)S(1)} %get-tuple-element.117, s32[]{:T(128)} %get-tuple-element.116, bf16[4,128,512]{2,1,0:T(8,128)(2,1)} %get-tuple-element.128, bf16[8,4,32,128]{3,1,2,0:T(4,128)(2,1)S(1)} %convolution_convert_fusion.2), kind=kOutput, calls=%fused_computation.5.clone.1 | convolution fusion | flops 134348800 | bytes 1048580 | tf_op jit(solution)/shard_map/while/body/eval_jaxpr/uwck,wkp->ucp/dot_general | solution.py:142
  21.8 1.3 %fusion.280 = bf16[8,8,32,512]{3,2,1,0:T(8,128)(2,1)S(1)} fusion(bf16[8,8,32,512]{3,2,1,0:T(8,128)(2,1)S(1)} %get-tuple-element.117, s32[]{:T(128)} %get-tuple-element.116, bf16[4,128,512]{2,1,0:T(8,128)(2,1)} %get-tuple-element.128, bf16[8,4,32,128]{3,1,2,0:T(4,128)(2,1)S(1)} %convolution_convert_fusion.2), kind=kOutput, calls=%fused_computation.5.clone.1 | convolution fusion | flops 134348800 | bytes 1048580 | tf_op jit(solution)/shard_map/while/body/eval_jaxpr/uwck,wkp->ucp/dot_general | solution.py:142
  23.4 0.6 gather_fusion
  24.4 1.3 %fusion.280 = bf16[8,8,32,512]{3,2,1,0:T(8,128)(2,1)S(1)} fusion(bf16[8,8,32,512]{3,2,1,0:T(8,128)(2,1)S(1)} %get-tuple-element.117, s32[]{:T(128)} %get-tuple-element.116, bf16[4,128,512]{2,1,0:T(8,128)(2,1)} %get-tuple-element.128, bf16[8,4,32,128]{3,1,2,0:T(4,128)(2,1)S(1)} %convolution_convert_fusion.2), kind=kOutput, calls=%fused_computation.5.clone.1 | convolution fusion | flops 134348800 | bytes 1048580 | tf_op jit(solution)/shard_map/while/body/eval_jaxpr/uwck,wkp->ucp/dot_general | solution.py:142
  27.0 1.3 %fusion.280 = bf16[8,8,32,512]{3,2,1,0:T(8,128)(2,1)S(1)} fusion(bf16[8,8,32,512]{3,2,1,0:T(8,128)(2,1)S(1)} %get-tuple-element.117, s32[]{:T(128)} %get-tuple-element.116, bf16[4,128,512]{2,1,0:T(8,128)(2,1)} %get-tuple-element.128, bf16[8,4,32,128]{3,1,2,0:T(4,128)(2,1)S(1)} %convolution_convert_fusion.2), kind=kOutput, calls=%fused_computation.5.clone.1 | convolution fusion | flops 134348800 | bytes 1048580 | tf_op jit(solution)/shard_map/while/body/eval_jaxpr/uwck,wkp->ucp/dot_general | solution.py:142
  28.6 0.6 gather_fusion
  29.6 1.3 %fusion.280 = bf16[8,8,32,512]{3,2,1,0:T(8,128)(2,1)S(1)} fusion(bf16[8,8,32,512]{3,2,1,0:T(8,128)(2,1)S(1)} %get-tuple-element.117, s32[]{:T(128)} %get-tuple-element.116, bf16[4,128,512]{2,1,0:T(8,128)(2,1)} %get-tuple-element.128, bf16[8,4,32,128]{3,1,2,0:T(4,128)(2,1)S(1)} %convolution_convert_fusion.2), kind=kOutput, calls=%fused_computation.5.clone.1 | convolution fusion | flops 134348800 | bytes 1048580 | tf_op jit(solution)/shard_map/while/body/eval_jaxpr/uwck,wkp->ucp/dot_general | solution.py:142
  31.3 3.0 %reshape.224 = f32[64,8,4,512]{3,2,1,0:T(4,128)} reshape(bf16[8,8,32,512]{3,2,1,0:T(8,128)(2,1)S(1)} %get-tuple-element.37) | data formatting | bytes 6291456 | tf_op jit(solution)/shard_map/convert_element_type | solution.py:149
  34.5 2.3 %collective-permute-start.5 = (bf16[1,1,32,512]{3,2,1,0:T(8,128)(2,1)S(1)}, bf16[1,1,32,512]{3,2,1,0:T(8,128)(2,1)S(1)}, u32[]{:S(2)}, u32[]{:S(2)}) collective-permute-start(bf16[1,1,32,512]{3,2,1,0:T(8,128)(2,1)S(1)} %bitcast.555), channel_id=1, source_target_pairs={{0,6},{1,7},{2,8},{3,9},{4,10},{5,11},{6,12},{7,13},{8,14},{9,15},... | collective-permute-start | bytes 98312 | tf_op jit(solution)/shard_map/ppermute | solution.py:32
  37.0 0.6 collective-permute-start.7
  37.6 2.5 %collective-permute-start.8 = (bf16[1,1,32,512]{3,2,1,0:T(8,128)(2,1)S(1)}, bf16[1,1,32,512]{3,2,1,0:T(8,128)(2,1)S(1)}, u32[]{:S(2)}, u32[]{:S(2)}) collective-permute-start(bf16[1,1,32,512]{3,2,1,0:T(8,128)(2,1)S(1)} %bitcast.559), channel_id=1, source_target_pairs={{0,9},{1,10},{2,11},{3,12},{4,13},{5,14},{6,15},{7,0},{8,1},{9,2},... | collective-permute-start | bytes 98312 | tf_op jit(solution)/shard_map/ppermute | solution.py:32
  40.1 2.4 %collective-permute-start.9 = (bf16[1,1,32,512]{3,2,1,0:T(8,128)(2,1)S(1)}, bf16[1,1,32,512]{3,2,1,0:T(8,128)(2,1)S(1)}, u32[]{:S(2)}, u32[]{:S(2)}) collective-permute-start(bf16[1,1,32,512]{3,2,1,0:T(8,128)(2,1)S(1)} %bitcast.560), channel_id=1, source_target_pairs={{0,10},{1,11},{2,12},{3,13},{4,14},{5,15},{6,0},{7,1},{8,2},{9,3},... | collective-permute-start | bytes 98312 | tf_op jit(solution)/shard_map/ppermute | solution.py:32
  42.6 1.5 %collective-permute-start.11 = (bf16[1,1,32,512]{3,2,1,0:T(8,128)(2,1)S(1)}, bf16[1,1,32,512]{3,2,1,0:T(8,128)(2,1)S(1)}, u32[]{:S(2)}, u32[]{:S(2)}) collective-permute-start(bf16[1,1,32,512]{3,2,1,0:T(8,128)(2,1)S(1)} %bitcast.562), channel_id=1, source_target_pairs={{0,12},{1,13},{2,14},{3,15},{4,0},{5,1},{6,2},{7,3},{8,4},{9,5},{1... | collective-permute-start | bytes 98312 | tf_op jit(solution)/shard_map/ppermute | solution.py:32
  44.0 2.4 %collective-permute-start.12 = (bf16[1,1,32,512]{3,2,1,0:T(8,128)(2,1)S(1)}, bf16[1,1,32,512]{3,2,1,0:T(8,128)(2,1)S(1)}, u32[]{:S(2)}, u32[]{:S(2)}) collective-permute-start(bf16[1,1,32,512]{3,2,1,0:T(8,128)(2,1)S(1)} %bitcast.563), channel_id=1, source_target_pairs={{0,13},{1,14},{2,15},{3,0},{4,1},{5,2},{6,3},{7,4},{8,5},{9,6},{10... | collective-permute-start | bytes 98312 | tf_op jit(solution)/shard_map/ppermute | solution.py:32
  46.4 1.8 %collective-permute-start.13 = (bf16[1,1,32,512]{3,2,1,0:T(8,128)(2,1)S(1)}, bf16[1,1,32,512]{3,2,1,0:T(8,128)(2,1)S(1)}, u32[]{:S(2)}, u32[]{:S(2)}) collective-permute-start(bf16[1,1,32,512]{3,2,1,0:T(8,128)(2,1)S(1)} %bitcast.564), channel_id=1, source_target_pairs={{0,14},{1,15},{2,0},{3,1},{4,2},{5,3},{6,4},{7,5},{8,6},{9,7},{10,... | collective-permute-start | bytes 98312 | tf_op jit(solution)/shard_map/ppermute | solution.py:32
  48.5 1.7 %collective-permute-done.13 = bf16[1,1,32,512]{3,2,1,0:T(8,128)(2,1)S(1)} collective-permute-done((bf16[1,1,32,512]{3,2,1,0:T(8,128)(2,1)S(1)}, bf16[1,1,32,512]{3,2,1,0:T(8,128)(2,1)S(1)}, u32[]{:S(2)}, u32[]{:S(2)}) %collective-permute-start.13) | collective-permute-done | bytes 32800 | tf_op jit(solution)/shard_map/ppermute | solution.py:32
  50.1 2.3 %collective-permute-done.14 = bf16[1,1,32,512]{3,2,1,0:T(8,128)(2,1)S(1)} collective-permute-done((bf16[1,1,32,512]{3,2,1,0:T(8,128)(2,1)S(1)}, bf16[1,1,32,512]{3,2,1,0:T(8,128)(2,1)S(1)}, u32[]{:S(2)}, u32[]{:S(2)}) %collective-permute-start.14) | collective-permute-done | bytes 32800 | tf_op jit(solution)/shard_map/ppermute | solution.py:32
  52.5 2.5 %mul.20 = f32[16,4,32,512]{3,2,1,0:T(8,128)} broadcast(bf16[16,32,512]{2,1,0:T(8,128)(2,1)S(1)} %bitcast_dynamic-update-slice_fusion), dimensions={0,2,3} | broadcast | bytes 4718592 | tf_op jit(solution)/shard_map/mul | solution.py:149
  55.0 5.2 %mul.21 = f32[64,8,4,512]{3,2,1,0:T(4,128)} reshape(f32[16,4,32,512]{3,2,1,0:T(8,128)} %mul.20) | data formatting | bytes 8388608 | tf_op jit(solution)/shard_map/mul | solution.py:149
  60.2 7.3 %multiply_reduce_fusion = f32[64,8,512]{2,1,0:T(8,128)S(1)} fusion(f32[64,8,4,512]{3,2,1,0:T(4,128)} %mul.21, f32[64,8,4,512]{3,2,1,0:T(4,128)} %reshape.224), kind=kLoop, calls=%fused_computation.19 | loop fusion | flops 1835008 | bytes 9437184 | tf_op jit(solution)/shard_map/reduce_sum | solution.py:151
  68.2 1.0 pad_maximum_fusion
  69.2 6.3 %all-to-all-start = ((bf16[16,4,4224]{2,1,0:T(4,128)(2,1)}), bf16[16,4,4224]{2,1,0:T(4,128)(2,1)S(1)}, u32[]{:S(2)}, u32[]{:S(2)}) async-start(bf16[16,4,4224]{2,1,0:T(4,128)(2,1)} %pad_maximum_fusion), calls=%async_computation | async-start | bytes 1081344 | tf_op jit(solution)/shard_map/all_to_all | solution.py:157
  75.5 14.0 %all-to-all-done = bf16[16,4,4224]{2,1,0:T(4,128)(2,1)S(1)} async-done(((bf16[16,4,4224]{2,1,0:T(4,128)(2,1)}), bf16[16,4,4224]{2,1,0:T(4,128)(2,1)S(1)}, u32[]{:S(2)}, u32[]{:S(2)}) %all-to-all-start) | async-done | bytes 540704 | tf_op jit(solution)/shard_map/all_to_all | solution.py:157
  90.8 3.6 %collective-permute-start.15 = (bf16[1,8,64,128]{3,1,2,0:T(8,128)(2,1)S(1)}, bf16[1,8,64,128]{3,1,2,0:T(8,128)(2,1)S(1)}, u32[]{:S(2)}, u32[]{:S(2)}) collective-permute-start(bf16[1,8,64,128]{3,1,2,0:T(8,128)(2,1)S(1)} %get-tuple-element.70), channel_id=1, source_target_pairs={{0,1},{1,2},{2,3},{3,4},{4,5},{5,6},{6,7},{7,8},{8,9},{9,10},{10,1... | collective-permute-start | bytes 393224 | tf_op jit(solution)/shard_map/ppermute | solution.py:44
  94.4 2.1 %collective-permute-start.16 = (bf16[1,8,64,128]{3,1,2,0:T(8,128)(2,1)S(1)}, bf16[1,8,64,128]{3,1,2,0:T(8,128)(2,1)S(1)}, u32[]{:S(2)}, u32[]{:S(2)}) collective-permute-start(bf16[1,8,64,128]{3,1,2,0:T(8,128)(2,1)S(1)} %get-tuple-element.71), channel_id=1, source_target_pairs={{1,0},{2,1},{3,2},{4,3},{5,4},{6,5},{7,6},{8,7},{9,8},{10,9},{11,1... | collective-permute-start | bytes 393224 | tf_op jit(solution)/shard_map/ppermute | solution.py:47
  96.9 4.7 %collective-permute-done.16 = bf16[1,8,64,128]{3,1,2,0:T(8,128)(2,1)S(1)} collective-permute-done((bf16[1,8,64,128]{3,1,2,0:T(8,128)(2,1)S(1)}, bf16[1,8,64,128]{3,1,2,0:T(8,128)(2,1)S(1)}, u32[]{:S(2)}, u32[]{:S(2)}) %collective-permute-start.16) | collective-permute-done | bytes 131104 | tf_op jit(solution)/shard_map/ppermute | solution.py:47
  101.6 1.5 %fusion.17 = bf16[6,8,66,130]{3,1,2,0:T(8,128)(2,1)S(1)} fusion(bf16[1,8,64,128]{3,1,2,0:T(8,128)(2,1)S(1)} %collective-permute-done.16, bf16[4,8,64,128]{3,1,2,0:T(8,128)(2,1)S(1)} %bitcast.516, bf16[1,8,64,128]{3,1,2,0:T(8,128)(2,1)S(1)} %collective-permute-done.15), kind=kLoop, calls=%fused_computation.32 | loop fusion | flops 7824960 | bytes 1610112 | tf_op jit(solution)/shard_map/concatenate | solution.py:48
  111.2 0.9 fusion.42
  112.5 0.8 fusion.44
  113.3 1.9 %collective-permute-start.17 = (bf16[1,8,64,128]{3,1,2,0:T(8,128)(2,1)S(1)}, bf16[1,8,64,128]{3,1,2,0:T(8,128)(2,1)S(1)}, u32[]{:S(2)}, u32[]{:S(2)}) collective-permute-start(bf16[1,8,64,128]{3,1,2,0:T(8,128)(2,1)S(1)} %get-tuple-element.68), channel_id=1, source_target_pairs={{0,1},{1,2},{2,3},{3,4},{4,5},{5,6},{6,7},{7,8},{8,9},{9,10},{10,1... | collective-permute-start | bytes 393224 | tf_op jit(solution)/shard_map/ppermute | solution.py:44
  115.2 2.6 %collective-permute-start.18 = (bf16[1,8,64,128]{3,1,2,0:T(8,128)(2,1)S(1)}, bf16[1,8,64,128]{3,1,2,0:T(8,128)(2,1)S(1)}, u32[]{:S(2)}, u32[]{:S(2)}) collective-permute-start(bf16[1,8,64,128]{3,1,2,0:T(8,128)(2,1)S(1)} %get-tuple-element.69), channel_id=1, source_target_pairs={{1,0},{2,1},{3,2},{4,3},{5,4},{6,5},{7,6},{8,7},{9,8},{10,9},{11,1... | collective-permute-start | bytes 393224 | tf_op jit(solution)/shard_map/ppermute | solution.py:47
  118.2 4.2 %collective-permute-done.18 = bf16[1,8,64,128]{3,1,2,0:T(8,128)(2,1)S(1)} collective-permute-done((bf16[1,8,64,128]{3,1,2,0:T(8,128)(2,1)S(1)}, bf16[1,8,64,128]{3,1,2,0:T(8,128)(2,1)S(1)}, u32[]{:S(2)}, u32[]{:S(2)}) %collective-permute-start.18) | collective-permute-done | bytes 131104 | tf_op jit(solution)/shard_map/ppermute | solution.py:47
  122.4 1.5 %select_maximum_fusion = bf16[6,8,66,130]{3,1,2,0:T(8,128)(2,1)S(1)} fusion(bf16[1,8,64,128]{3,1,2,0:T(8,128)(2,1)S(1)} %collective-permute-done.18, bf16[4,8,64,128]{3,1,2,0:T(8,128)(2,1)S(1)} %fusion.44, bf16[1,8,64,128]{3,1,2,0:T(8,128)(2,1)S(1)} %collective-permute-done.17), kind=kLoop, calls=%fused_computation.23 | loop fusion | flops 7824960 | bytes 1610112 | tf_op jit(solution)/shard_map/concatenate | solution.py:48
  132.4 0.9 add_add_fusion
  (191 shorter events, 27.4 us)
Async XLA Ops:
  0.0 8.6 %copy-start.3 = (s32[1,64,4]{1,2,0:T(4,128)S(1)}, s32[1,64,4]{1,2,0:T(4,128)}, u32[]{:S(2)}) copy-start(s32[1,64,4]{1,2,0:T(4,128)} %param.15) | copy-start | bytes 3076
  0.0 9.2 %copy-start.6 = (s32[1,64]{1,0:T(1,128)S(1)}, s32[1,64]{1,0:T(1,128)}, u32[]{:S(2)}) copy-start(s32[1,64]{1,0:T(1,128)} %param.16) | copy-start | bytes 772
  0.0 10.0 %copy-start.4 = (s32[1,64,4]{1,2,0:T(4,128)S(1)}, s32[1,64,4]{1,2,0:T(4,128)}, u32[]{:S(2)}) copy-start(s32[1,64,4]{1,2,0:T(4,128)} %param.14) | copy-start | bytes 3076
  0.0 34.5 %collective-permute-start = (bf16[1,1,32,512]{3,2,1,0:T(8,128)(2,1)}, bf16[1,1,32,512]{3,2,1,0:T(8,128)(2,1)S(1)}, u32[]{:S(2)}, u32[]{:S(2)}) collective-permute-start(bf16[1,1,32,512]{3,2,1,0:T(8,128)(2,1)} %bitcast.550), channel_id=1, source_target_pairs={{0,1},{1,2},{2,3},{3,4},{4,5},{5,6},{6,7},{7,8},{8,9},{9,10},{10,1... | collective-permute-start | bytes 98312 | tf_op jit(solution)/shard_map/ppermute | solution.py:32
  1.9 35.0 %collective-permute-start.1 = (bf16[1,1,32,512]{3,2,1,0:T(8,128)(2,1)}, bf16[1,1,32,512]{3,2,1,0:T(8,128)(2,1)S(1)}, u32[]{:S(2)}, u32[]{:S(2)}) collective-permute-start(bf16[1,1,32,512]{3,2,1,0:T(8,128)(2,1)} %bitcast.551), channel_id=1, source_target_pairs={{0,2},{1,3},{2,4},{3,5},{4,6},{5,7},{6,8},{7,9},{8,10},{9,11},{10,... | collective-permute-start | bytes 98312 | tf_op jit(solution)/shard_map/ppermute | solution.py:32
  3.1 33.9 %collective-permute-start.2 = (bf16[1,1,32,512]{3,2,1,0:T(8,128)(2,1)}, bf16[1,1,32,512]{3,2,1,0:T(8,128)(2,1)S(1)}, u32[]{:S(2)}, u32[]{:S(2)}) collective-permute-start(bf16[1,1,32,512]{3,2,1,0:T(8,128)(2,1)} %bitcast.552), channel_id=1, source_target_pairs={{0,3},{1,4},{2,5},{3,6},{4,7},{5,8},{6,9},{7,10},{8,11},{9,12},{10... | collective-permute-start | bytes 98312 | tf_op jit(solution)/shard_map/ppermute | solution.py:32
  3.5 34.1 %collective-permute-start.3 = (bf16[1,1,32,512]{3,2,1,0:T(8,128)(2,1)}, bf16[1,1,32,512]{3,2,1,0:T(8,128)(2,1)S(1)}, u32[]{:S(2)}, u32[]{:S(2)}) collective-permute-start(bf16[1,1,32,512]{3,2,1,0:T(8,128)(2,1)} %bitcast.553), channel_id=1, source_target_pairs={{0,4},{1,5},{2,6},{3,7},{4,8},{5,9},{6,10},{7,11},{8,12},{9,13},{1... | collective-permute-start | bytes 98312 | tf_op jit(solution)/shard_map/ppermute | solution.py:32
  4.4 35.7 %collective-permute-start.4 = (bf16[1,1,32,512]{3,2,1,0:T(8,128)(2,1)}, bf16[1,1,32,512]{3,2,1,0:T(8,128)(2,1)S(1)}, u32[]{:S(2)}, u32[]{:S(2)}) collective-permute-start(bf16[1,1,32,512]{3,2,1,0:T(8,128)(2,1)} %bitcast.554), channel_id=1, source_target_pairs={{0,5},{1,6},{2,7},{3,8},{4,9},{5,10},{6,11},{7,12},{8,13},{9,14},{... | collective-permute-start | bytes 98312 | tf_op jit(solution)/shard_map/ppermute | solution.py:32
  10.1 20.8 %copy-start.5 = (s32[1,64]{1,0:T(1,128)S(1)}, s32[1,64]{1,0:T(1,128)}, u32[]{:S(2)}) copy-start(s32[1,64]{1,0:T(1,128)} %param.17) | copy-start | bytes 772
  31.3 3.2 %copy-start.2 = (bf16[1,32,512]{2,1,0:T(8,128)(2,1)S(1)}, bf16[1,32,512]{2,1,0:T(8,128)(2,1)}, u32[]{:S(2)}) copy-start(bf16[1,32,512]{2,1,0:T(8,128)(2,1)} %param.12) | copy-start | bytes 98308
  34.5 8.0 %collective-permute-start.5 = (bf16[1,1,32,512]{3,2,1,0:T(8,128)(2,1)S(1)}, bf16[1,1,32,512]{3,2,1,0:T(8,128)(2,1)S(1)}, u32[]{:S(2)}, u32[]{:S(2)}) collective-permute-start(bf16[1,1,32,512]{3,2,1,0:T(8,128)(2,1)S(1)} %bitcast.555), channel_id=1, source_target_pairs={{0,6},{1,7},{2,8},{3,9},{4,10},{5,11},{6,12},{7,13},{8,14},{9,15},... | collective-permute-start | bytes 98312 | tf_op jit(solution)/shard_map/ppermute | solution.py:32
  36.9 5.7 %collective-permute-start.6 = (bf16[1,1,32,512]{3,2,1,0:T(8,128)(2,1)S(1)}, bf16[1,1,32,512]{3,2,1,0:T(8,128)(2,1)S(1)}, u32[]{:S(2)}, u32[]{:S(2)}) collective-permute-start(bf16[1,1,32,512]{3,2,1,0:T(8,128)(2,1)S(1)} %bitcast.557), channel_id=1, source_target_pairs={{0,7},{1,8},{2,9},{3,10},{4,11},{5,12},{6,13},{7,14},{8,15},{9,0},... | collective-permute-start | bytes 98312 | tf_op jit(solution)/shard_map/ppermute | solution.py:32
  37.0 7.0 %collective-permute-start.7 = (bf16[1,1,32,512]{3,2,1,0:T(8,128)(2,1)S(1)}, bf16[1,1,32,512]{3,2,1,0:T(8,128)(2,1)S(1)}, u32[]{:S(2)}, u32[]{:S(2)}) collective-permute-start(bf16[1,1,32,512]{3,2,1,0:T(8,128)(2,1)S(1)} %bitcast.558), channel_id=1, source_target_pairs={{0,8},{1,9},{2,10},{3,11},{4,12},{5,13},{6,14},{7,15},{8,0},{9,1},... | collective-permute-start | bytes 98312 | tf_op jit(solution)/shard_map/ppermute | solution.py:32
  37.6 8.8 %collective-permute-start.8 = (bf16[1,1,32,512]{3,2,1,0:T(8,128)(2,1)S(1)}, bf16[1,1,32,512]{3,2,1,0:T(8,128)(2,1)S(1)}, u32[]{:S(2)}, u32[]{:S(2)}) collective-permute-start(bf16[1,1,32,512]{3,2,1,0:T(8,128)(2,1)S(1)} %bitcast.559), channel_id=1, source_target_pairs={{0,9},{1,10},{2,11},{3,12},{4,13},{5,14},{6,15},{7,0},{8,1},{9,2},... | collective-permute-start | bytes 98312 | tf_op jit(solution)/shard_map/ppermute | solution.py:32
  40.1 8.1 %collective-permute-start.9 = (bf16[1,1,32,512]{3,2,1,0:T(8,128)(2,1)S(1)}, bf16[1,1,32,512]{3,2,1,0:T(8,128)(2,1)S(1)}, u32[]{:S(2)}, u32[]{:S(2)}) collective-permute-start(bf16[1,1,32,512]{3,2,1,0:T(8,128)(2,1)S(1)} %bitcast.560), channel_id=1, source_target_pairs={{0,10},{1,11},{2,12},{3,13},{4,14},{5,15},{6,0},{7,1},{8,2},{9,3},... | collective-permute-start | bytes 98312 | tf_op jit(solution)/shard_map/ppermute | solution.py:32
  42.5 5.8 %collective-permute-start.10 = (bf16[1,1,32,512]{3,2,1,0:T(8,128)(2,1)S(1)}, bf16[1,1,32,512]{3,2,1,0:T(8,128)(2,1)S(1)}, u32[]{:S(2)}, u32[]{:S(2)}) collective-permute-start(bf16[1,1,32,512]{3,2,1,0:T(8,128)(2,1)S(1)} %bitcast.561), channel_id=1, source_target_pairs={{0,11},{1,12},{2,13},{3,14},{4,15},{5,0},{6,1},{7,2},{8,3},{9,4},{... | collective-permute-start | bytes 98312 | tf_op jit(solution)/shard_map/ppermute | solution.py:32
  42.6 5.7 %collective-permute-start.11 = (bf16[1,1,32,512]{3,2,1,0:T(8,128)(2,1)S(1)}, bf16[1,1,32,512]{3,2,1,0:T(8,128)(2,1)S(1)}, u32[]{:S(2)}, u32[]{:S(2)}) collective-permute-start(bf16[1,1,32,512]{3,2,1,0:T(8,128)(2,1)S(1)} %bitcast.562), channel_id=1, source_target_pairs={{0,12},{1,13},{2,14},{3,15},{4,0},{5,1},{6,2},{7,3},{8,4},{9,5},{1... | collective-permute-start | bytes 98312 | tf_op jit(solution)/shard_map/ppermute | solution.py:32
  44.0 4.4 %collective-permute-start.12 = (bf16[1,1,32,512]{3,2,1,0:T(8,128)(2,1)S(1)}, bf16[1,1,32,512]{3,2,1,0:T(8,128)(2,1)S(1)}, u32[]{:S(2)}, u32[]{:S(2)}) collective-permute-start(bf16[1,1,32,512]{3,2,1,0:T(8,128)(2,1)S(1)} %bitcast.563), channel_id=1, source_target_pairs={{0,13},{1,14},{2,15},{3,0},{4,1},{5,2},{6,3},{7,4},{8,5},{9,6},{10... | collective-permute-start | bytes 98312 | tf_op jit(solution)/shard_map/ppermute | solution.py:32
  46.4 3.7 %collective-permute-start.13 = (bf16[1,1,32,512]{3,2,1,0:T(8,128)(2,1)S(1)}, bf16[1,1,32,512]{3,2,1,0:T(8,128)(2,1)S(1)}, u32[]{:S(2)}, u32[]{:S(2)}) collective-permute-start(bf16[1,1,32,512]{3,2,1,0:T(8,128)(2,1)S(1)} %bitcast.564), channel_id=1, source_target_pairs={{0,14},{1,15},{2,0},{3,1},{4,2},{5,3},{6,4},{7,5},{8,6},{9,7},{10,... | collective-permute-start | bytes 98312 | tf_op jit(solution)/shard_map/ppermute | solution.py:32
  48.2 4.3 %collective-permute-start.14 = (bf16[1,1,32,512]{3,2,1,0:T(8,128)(2,1)S(1)}, bf16[1,1,32,512]{3,2,1,0:T(8,128)(2,1)S(1)}, u32[]{:S(2)}, u32[]{:S(2)}) collective-permute-start(bf16[1,1,32,512]{3,2,1,0:T(8,128)(2,1)S(1)} %bitcast.565), channel_id=1, source_target_pairs={{0,15},{1,0},{2,1},{3,2},{4,3},{5,4},{6,5},{7,6},{8,7},{9,8},{10,9... | collective-permute-start | bytes 98312 | tf_op jit(solution)/shard_map/ppermute | solution.py:32
  69.2 20.3 %all-to-all-start = ((bf16[16,4,4224]{2,1,0:T(4,128)(2,1)}), bf16[16,4,4224]{2,1,0:T(4,128)(2,1)S(1)}, u32[]{:S(2)}, u32[]{:S(2)}) async-start(bf16[16,4,4224]{2,1,0:T(4,128)(2,1)} %pad_maximum_fusion), calls=%async_computation | async-start | bytes 1081344 | tf_op jit(solution)/shard_map/all_to_all | solution.py:157
  90.3 6.2 %copy-start.1 = (bf16[3,3,3,8,8]{4,3,2,1,0:T(8,128)(2,1)S(1)}, bf16[3,3,3,8,8]{4,3,2,1,0:T(8,128)(2,1)}, u32[]{:S(2)}) copy-start(bf16[3,3,3,8,8]{4,3,2,1,0:T(8,128)(2,1)} %param.18) | copy-start | bytes 10372
  90.8 6.1 %collective-permute-start.15 = (bf16[1,8,64,128]{3,1,2,0:T(8,128)(2,1)S(1)}, bf16[1,8,64,128]{3,1,2,0:T(8,128)(2,1)S(1)}, u32[]{:S(2)}, u32[]{:S(2)}) collective-permute-start(bf16[1,8,64,128]{3,1,2,0:T(8,128)(2,1)S(1)} %get-tuple-element.70), channel_id=1, source_target_pairs={{0,1},{1,2},{2,3},{3,4},{4,5},{5,6},{6,7},{7,8},{8,9},{9,10},{10,1... | collective-permute-start | bytes 393224 | tf_op jit(solution)/shard_map/ppermute | solution.py:44
  94.4 7.2 %collective-permute-start.16 = (bf16[1,8,64,128]{3,1,2,0:T(8,128)(2,1)S(1)}, bf16[1,8,64,128]{3,1,2,0:T(8,128)(2,1)S(1)}, u32[]{:S(2)}, u32[]{:S(2)}) collective-permute-start(bf16[1,8,64,128]{3,1,2,0:T(8,128)(2,1)S(1)} %get-tuple-element.71), channel_id=1, source_target_pairs={{1,0},{2,1},{3,2},{4,3},{5,4},{6,5},{7,6},{8,7},{9,8},{10,9},{11,1... | collective-permute-start | bytes 393224 | tf_op jit(solution)/shard_map/ppermute | solution.py:47
  112.5 5.4 %copy-start = (bf16[3,3,3,8]{3,2,1,0:T(4,128)(2,1)S(1)}, bf16[3,3,3,8]{3,2,1,0:T(4,128)(2,1)}, u32[]{:S(2)}) copy-start(bf16[3,3,3,8]{3,2,1,0:T(4,128)(2,1)} %param.19) | copy-start | bytes 1300
  113.3 4.9 %collective-permute-start.17 = (bf16[1,8,64,128]{3,1,2,0:T(8,128)(2,1)S(1)}, bf16[1,8,64,128]{3,1,2,0:T(8,128)(2,1)S(1)}, u32[]{:S(2)}, u32[]{:S(2)}) collective-permute-start(bf16[1,8,64,128]{3,1,2,0:T(8,128)(2,1)S(1)} %get-tuple-element.68), channel_id=1, source_target_pairs={{0,1},{1,2},{2,3},{3,4},{4,5},{5,6},{6,7},{7,8},{8,9},{9,10},{10,1... | collective-permute-start | bytes 393224 | tf_op jit(solution)/shard_map/ppermute | solution.py:44
  115.2 7.2 %collective-permute-start.18 = (bf16[1,8,64,128]{3,1,2,0:T(8,128)(2,1)S(1)}, bf16[1,8,64,128]{3,1,2,0:T(8,128)(2,1)S(1)}, u32[]{:S(2)}, u32[]{:S(2)}) collective-permute-start(bf16[1,8,64,128]{3,1,2,0:T(8,128)(2,1)S(1)} %get-tuple-element.69), channel_id=1, source_target_pairs={{1,0},{2,1},{3,2},{4,3},{5,4},{6,5},{7,6},{8,7},{9,8},{10,9},{11,1... | collective-permute-start | bytes 393224 | tf_op jit(solution)/shard_map/ppermute | solution.py:47
